TPU v7x, 128 devices: a whole 4x4x4 slice. The times are simulated.
128 devices in a mesh: seq: 16 (over z, x_lo, core), chan: 4 (over y), rep: 2 (over x_hi).
Axes of the slice: x: 4 (x_hi: 2, x_lo: 2; x = x_hi * 2 + x_lo), y: 4, z: 4, core: 2. Of those that a mesh axis runs over, the one named last changes fastest.
Arguments:
- inputs: bfloat16 [2, 4096, 2048], P('rep', 'seq', 'chan'), may hold values from -6 to 6
- w_in: bfloat16 [2048, 1536], P('chan'), may hold values from -0.25 to 0.25
- w_out: bfloat16 [2048, 2048], P('chan'), may hold values from -0.125 to 0.125
- filt_fwd: float32 [4096, 2048], P('seq', 'chan'), may hold values from -0.09375 to 0.09375
- filt_bwd: float32 [4096, 2048], P('seq', 'chan'), may hold values from -0.09375 to 0.09375
- skip_gain: float32 [2048], P('chan'), may hold values from -4 to 4
- cotangent: bfloat16 [2, 4096, 2048], P('rep', 'seq', 'chan'), may hold values from -6 to 6
Outputs:
- layer_out: bfloat16 [2, 4096, 2048], P('rep', 'seq', 'chan')
- d_input: bfloat16 [2, 4096, 2048], P('rep', 'seq', 'chan')
- d_w_in: float32 [2048, 1536], P('chan')
- d_w_out: float32 [2048, 2048], P('chan')
- d_filt_fwd: float32 [4096, 2048], P('seq', 'chan')
- d_filt_bwd: float32 [4096, 2048], P('seq', 'chan')
- d_skip: float32 [2048], P('chan')
All inputs are finite; a program needn't handle non-finite values.
Results may differ from a plain program's by a relative error of at most 0.005.
Values may be sent and summed in bfloat16 or wider, within the bound.
No kernel may reach another device: no remote copies, remote signals or barrier semaphores. Data moves between devices by JAX's collectives and lax.ppermute only.
A program may use at most 128 MiB of HBM per device.

v0:
```python
import math
import jax
import jax.numpy as jnp
from jax import lax
from jax.sharding import PartitionSpec as P

BLOCK = 512
HIGHEST_PRECISION = lax.Precision.HIGHEST


def wrapped_angle(phase, modulus, factor):
    centered = jnp.where(phase * 2 > modulus, phase - modulus, phase)
    return factor * math.pi / modulus * centered.astype(jnp.float32)


def unit_tables(table_size):
    index_row = jnp.arange(table_size, dtype=jnp.int32)
    phase = index_row[:, None] * index_row[None, :] % table_size
    angle = wrapped_angle(phase, table_size, 2.0)
    return (jnp.cos(angle), jnp.sin(angle))


def table_apply(table, fields, form):
    return jnp.einsum(form, table, fields, precision=HIGHEST_PRECISION)


def rotate(real_part, imag_part, angle):
    cosine = jnp.cos(angle)
    sine = jnp.sin(angle)
    return (real_part * cosine - imag_part * sine, real_part * sine + imag_part * cosine)


def complex_product(left_re, left_im, right_re, right_im):
    return (left_re * right_re - left_im * right_im, left_re * right_im + left_im * right_re)


def regroup(stacked):
    return lax.all_to_all(stacked, "seq", split_axis=1, concat_axis=1, tiled=True)


def forward_transform(fields):
    part_count = lax.axis_size("seq")
    position = lax.axis_index("seq")
    field_count, row_count, chan_width = fields.shape
    block_rows = row_count // part_count
    seq_length = row_count * part_count
    columns = regroup(fields).reshape(field_count, part_count, block_rows, chan_width)
    cos_part, sin_part = unit_tables(part_count)
    real_part = table_apply(cos_part, columns, "kp,fpbc->fkbc")
    imag_part = -table_apply(sin_part, columns, "kp,fpbc->fkbc")
    offsets = position * block_rows + jnp.arange(block_rows, dtype=jnp.int32)
    phase = jnp.arange(part_count, dtype=jnp.int32)[:, None] * offsets[None, :] % seq_length
    angle = wrapped_angle(phase, seq_length, -2.0)
    real_part, imag_part = rotate(real_part, imag_part, angle[None, :, :, None])
    merged = jnp.concatenate([real_part, imag_part], axis=0).reshape(
        2 * field_count, row_count, chan_width
    )
    spread = regroup(merged)
    real_part = spread[:field_count]
    imag_part = spread[field_count:]
    cos_rows, sin_rows = unit_tables(row_count)
    spec_re = table_apply(cos_rows, real_part, "kb,fbc->fkc") + table_apply(
        sin_rows, imag_part, "kb,fbc->fkc"
    )
    spec_im = table_apply(cos_rows, imag_part, "kb,fbc->fkc") - table_apply(
        sin_rows, real_part, "kb,fbc->fkc"
    )
    return (spec_re, spec_im)


def inverse_transform(spec_re, spec_im):
    part_count = lax.axis_size("seq")
    position = lax.axis_index("seq")
    field_count, row_count, chan_width = spec_re.shape
    block_rows = row_count // part_count
    seq_length = row_count * part_count
    cos_rows, sin_rows = unit_tables(row_count)
    time_re = table_apply(cos_rows, spec_re, "bk,fkc->fbc") - table_apply(
        sin_rows, spec_im, "bk,fkc->fbc"
    )
    time_im = table_apply(cos_rows, spec_im, "bk,fkc->fbc") + table_apply(
        sin_rows, spec_re, "bk,fkc->fbc"
    )
    phase = position * jnp.arange(row_count, dtype=jnp.int32) % seq_length
    angle = wrapped_angle(phase, seq_length, 2.0)
    time_re, time_im = rotate(time_re, time_im, angle[None, :, None])
    merged = jnp.concatenate([time_re, time_im], axis=0)
    spread = regroup(merged).reshape(2 * field_count, part_count, block_rows, chan_width)
    cos_part, sin_part = unit_tables(part_count)
    result = table_apply(cos_part, spread[:field_count], "pk,fkbc->fpbc") - table_apply(
        sin_part, spread[field_count:], "pk,fkbc->fpbc"
    )
    settled = regroup(result.reshape(field_count, row_count, chan_width))
    return settled * (1.0 / seq_length)


def on_device(inputs, w_in, w_out, filt_fwd, filt_bwd, skip_gain, cotangent):
    input_rows = inputs[0]
    row_count, chan_width = input_rows.shape
    block_count = chan_width // BLOCK
    input_blocks = input_rows.reshape(row_count, block_count, BLOCK)
    w_blocks = w_in.reshape(block_count, BLOCK, 3, BLOCK)
    projected = jnp.einsum(
        "mni,nisj->smnj", input_blocks, w_blocks, preferred_element_type=jnp.float32
    )
    projected = projected.reshape(3, row_count, chan_width)
    keys, values, queries = (projected[0], projected[1], projected[2])
    mixed = keys * values
    spec_re, spec_im = forward_transform(jnp.stack([mixed, filt_fwd, filt_bwd]))
    mix_re, mix_im = (spec_re[0], spec_im[0])
    fwd_re, fwd_im = (spec_re[1], spec_im[1])
    bwd_re, bwd_im = (spec_re[2], spec_im[2])
    joint_re, joint_im = complex_product(fwd_re + bwd_re, fwd_im - bwd_im, mix_re, mix_im)
    long_conv = inverse_transform(joint_re[None], joint_im[None])[0]
    conv_out = long_conv + skip_gain * mixed
    gated = (queries * conv_out).astype(jnp.bfloat16)
    out_terms = jnp.dot(gated, w_out, preferred_element_type=jnp.float32)
    layer_out = lax.psum_scatter(out_terms, "chan", scatter_dimension=1, tiled=True).astype(
        jnp.bfloat16
    )
    grad_rows = cotangent[0]
    piece = lax.all_gather(grad_rows, "chan", axis=1, tiled=True)
    grad_gated = lax.dot_general(
        piece, w_out, (((1,), (1,)), ((), ())), preferred_element_type=jnp.float32
    )
    block_grad = lax.dot_general(
        gated, piece, (((0,), (0,)), ((), ())), preferred_element_type=jnp.float32
    )
    grad_wout = block_grad
    grad_gated, grad_wout = (grad_gated, grad_wout)
    grad_queries = grad_gated * conv_out
    grad_conv = grad_gated * queries
    grad_re, grad_im = forward_transform(grad_conv[None])
    grad_re, grad_im = (grad_re[0], grad_im[0])
    upper_re, upper_im = complex_product(fwd_re + bwd_re, bwd_im - fwd_im, grad_re, grad_im)
    cross_re, cross_im = complex_product(grad_re, grad_im, mix_re, -mix_im)
    results = inverse_transform(
        jnp.stack([upper_re, cross_re, cross_re]), jnp.stack([upper_im, cross_im, -cross_im])
    )
    back = results[0]
    grad_hfwd = results[-2]
    grad_hbwd = results[-1]
    grad_mixed = back + skip_gain * grad_conv
    grad_pre = jnp.stack([grad_mixed * values, grad_mixed * keys, grad_queries]).astype(
        jnp.bfloat16
    )
    pre_blocks = grad_pre.reshape(3, row_count, block_count, BLOCK)
    d_input = jnp.einsum("smnj,nisj->mni", pre_blocks, w_blocks, preferred_element_type=jnp.float32)
    d_input = d_input.reshape(row_count, chan_width).astype(jnp.bfloat16)
    grad_win = jnp.einsum(
        "mni,smnj->nisj", input_blocks, pre_blocks, preferred_element_type=jnp.float32
    )
    grad_win = grad_win.reshape(chan_width, 3 * BLOCK)
    grad_skip = jnp.sum(grad_conv * mixed, axis=0)
    grad_win, grad_wout, grad_skip = lax.psum((grad_win, grad_wout, grad_skip), ("seq", "rep"))
    grad_hfwd, grad_hbwd = lax.psum((grad_hfwd, grad_hbwd), "rep")
    scale = 1.0 / math.sqrt(lax.axis_size("rep") * lax.axis_size("seq") * row_count)
    return (
        layer_out[None],
        d_input[None],
        grad_win * scale,
        grad_wout * scale,
        grad_hfwd * scale,
        grad_hbwd * scale,
        grad_skip * scale,
    )


def solution(mesh):
    return jax.shard_map(
        on_device,
        mesh=mesh,
        in_specs=(
            P("rep", "seq", "chan"),
            P("chan", None),
            P("chan", None),
            P("seq", "chan"),
            P("seq", "chan"),
            P("chan"),
            P("rep", "seq", "chan"),
        ),
        out_specs=(
            P("rep", "seq", "chan"),
            P("rep", "seq", "chan"),
            P("chan", None),
            P("chan", None),
            P("seq", "chan"),
            P("seq", "chan"),
            P("chan"),
        ),
        check_vma=False,
    )
```

profile of v0, /device:TPU:1, one launch (start us, length us, event | category | flops | bytes accessed | tf_op | source)
XLA Modules:
  0.0 551.9 jit_solution(10543586648825998175)
XLA Ops:
  7.9 2.6 copy.79
  10.6 3.2 fusion.67
  13.8 21.2 %all-gather.3.cloned.1.call-done = bf16[1,256,2048]{2,1,0:T(8,128)(2,1)} async-done(((bf16[1,256,512]{2,1,0:T(8,128)(2,1)}), bf16[1,256,2048]{2,1,0:T(8,128)(2,1)}) %all-gather.3.cloned.1.call-update) | async-done | bytes 1048592 | tf_op jit(solution)/shard_map/all_gather | solution.py:122
  34.9 3.2 multiply_reduce_fusion
  39.2 8.1 %all-to-all-start.4 = ((f32[1,256,512]{2,0,1:T(1,128)}), f32[1,256,512]{2,0,1:T(1,128)S(1)}, u32[]{:S(2)}, u32[]{:S(2)}) async-start(f32[1,256,512]{2,0,1:T(1,128)} %copy.104), calls=%async_computation.5 | async-start | bytes 1048576 | tf_op jit(solution)/shard_map/all_to_all | solution.py:38
  47.3 2.0 copy.83
  49.3 2.0 copy.84
  54.1 2.9 copy.85
  57.0 5.7 %all-to-all-start = ((f32[3,256,512]{2,0,1:T(4,128)}), f32[3,256,512]{2,0,1:T(4,128)}, u32[]{:S(2)}, u32[]{:S(2)}) async-start(f32[3,256,512]{2,0,1:T(4,128)} %copy.85), calls=%async_computation | async-start | bytes 4194304 | tf_op jit(solution)/shard_map/all_to_all | solution.py:38
  65.7 1.8 copy.110
  67.5 22.3 %all-to-all-done = f32[3,256,512]{2,0,1:T(4,128)} async-done(((f32[3,256,512]{2,0,1:T(4,128)}), f32[3,256,512]{2,0,1:T(4,128)}, u32[]{:S(2)}, u32[]{:S(2)}) %all-to-all-start) | async-done | bytes 1572896 | tf_op jit(solution)/shard_map/all_to_all | solution.py:38
  89.8 5.7 %all-to-all-start.5 = ((f32[2,256,512]{2,0,1:T(2,128)}), f32[2,256,512]{2,0,1:T(2,128)}, u32[]{:S(2)}, u32[]{:S(2)}) async-start(f32[2,256,512]{2,0,1:T(2,128)} %copy.110), calls=%async_computation.6 | async-start | bytes 2097152 | tf_op jit(solution)/shard_map/all_to_all | solution.py:38
  95.5 2.1 copy.86
  97.6 2.5 fusion.9
  100.1 2.9 fusion
  103.5 1.8 copy.91
  105.4 3.9 copy.92
  109.3 1.9 all-to-all-done.5
  111.2 5.6 %all-to-all-start.1 = ((f32[6,256,512]{2,0,1:T(8,128)}), f32[6,256,512]{2,0,1:T(8,128)}, u32[]{:S(2)}, u32[]{:S(2)}) async-start(f32[6,256,512]{2,0,1:T(8,128)} %copy.92), calls=%async_computation.1 | async-start | bytes 8388608 | tf_op jit(solution)/shard_map/all_to_all | solution.py:38
  116.8 2.4 fusion.281
  119.3 1.8 fusion.30
  121.1 1.9 fusion.15
  123.0 2.6 fusion.26
  125.7 40.5 %all-to-all-done.1 = f32[6,256,512]{2,0,1:T(8,128)} async-done(((f32[6,256,512]{2,0,1:T(8,128)}), f32[6,256,512]{2,0,1:T(8,128)}, u32[]{:S(2)}, u32[]{:S(2)}) %all-to-all-start.1) | async-done | bytes 3145760 | tf_op jit(solution)/shard_map/all_to_all | solution.py:38
  166.2 6.6 %fusion.279 = (f32[3,256,512]{2,0,1:T(4,128)}, f32[3,256,512]{2,0,1:T(4,128)}) fusion(f32[6,256,512]{2,0,1:T(8,128)} %all-to-all-done.1), kind=kLoop, calls=%fused_computation.333 | loop fusion | bytes 6291456 | tf_op jit(solution)/shard_map/slice | solution.py:59
  172.8 2.7 copy.133
  175.5 2.9 copy.134
  178.4 4.0 fusion.63
  182.4 2.4 fusion.65
  184.8 2.5 subtract_bitcast_fusion.2
  187.4 2.5 add_bitcast_fusion.1
  189.9 3.8 fusion.277
  199.7 1.7 subtract_bitcast_fusion.3
  202.5 2.2 copy.95
  204.7 5.4 all-to-all-start.2
  210.1 3.9 fusion.11
  214.0 2.4 fusion.20
  216.5 2.5 convolution_add_fusion
  219.0 2.7 subtract_bitcast_fusion.1
  221.7 1.9 pad_maximum_fusion.1
  223.6 5.2 copy.111
  228.7 5.8 %all-to-all-start.6 = ((f32[6,256,512]{2,0,1:T(8,128)}), f32[6,256,512]{2,0,1:T(8,128)}, u32[]{:S(2)}, u32[]{:S(2)}) async-start(f32[6,256,512]{2,0,1:T(8,128)} %copy.111), calls=%async_computation.7 | async-start | bytes 8388608 | tf_op jit(solution)/shard_map/all_to_all | solution.py:38
  234.5 2.4 fusion.280
  240.5 43.5 %all-to-all-done.6 = f32[6,256,512]{2,0,1:T(8,128)} async-done(((f32[6,256,512]{2,0,1:T(8,128)}), f32[6,256,512]{2,0,1:T(8,128)}, u32[]{:S(2)}, u32[]{:S(2)}) %all-to-all-start.6) | async-done | bytes 3145760 | tf_op jit(solution)/shard_map/all_to_all | solution.py:38
  284.0 4.6 all-to-all-start.3
  288.7 4.5 fusion.278
  293.7 2.5 fusion.2
  296.7 2.6 subtract_bitcast_fusion
  300.2 2.4 copy.117
  302.6 5.8 %all-to-all-start.7 = ((f32[3,256,512]{2,0,1:T(4,128)}), f32[3,256,512]{2,0,1:T(4,128)}, u32[]{:S(2)}, u32[]{:S(2)}) async-start(f32[3,256,512]{2,0,1:T(4,128)} %copy.117), calls=%async_computation.8 | async-start | bytes 4194304 | tf_op jit(solution)/shard_map/all_to_all | solution.py:38
  309.6 25.8 %all-to-all-done.7 = f32[3,256,512]{2,0,1:T(4,128)} async-done(((f32[3,256,512]{2,0,1:T(4,128)}), f32[3,256,512]{2,0,1:T(4,128)}, u32[]{:S(2)}, u32[]{:S(2)}) %all-to-all-start.7) | async-done | bytes 1572896 | tf_op jit(solution)/shard_map/all_to_all | solution.py:38
  335.4 2.7 copy.118
  342.0 1.8 fusion.56
  345.2 2.2 convolution_bitcast_fusion
  347.4 2.7 fusion.21
  350.5 2.1 fusion.288
  352.6 69.5 %psum.39 = f32[512]{0:T(512)S(1)} all-reduce(f32[512]{0:T(512)S(1)} %get-tuple-element.32), channel_id=1, replica_groups=mesh['seq'=16,'chan'=4,'rep'=2] {'seq','rep'}, use_global_device_ids=true, to_apply=%region_6.7 | all-reduce | flops 512 | bytes 4096 | tf_op jit(solution)/shard_map/psum | solution.py:155
  422.7 2.8 fusion.19
  428.7 82.8 %all-reduce.5.cloned.1.call-done = (f32[512,1536]{0,1:T(8,128)}, f32[512,2048]{1,0:T(8,128)}) async-done(((f32[512,1536]{0,1:T(8,128)}, f32[512,2048]{1,0:T(8,128)}), (f32[512,1536]{0,1:T(8,128)}, f32[512,2048]{1,0:T(8,128)})) %all-reduce.5.cloned.1.call-update) | async-done | bytes 7340048 | tf_op jit(solution)/shard_map/psum | solution.py:155
  511.6 3.9 broadcast_multiply_fusion.1
  515.5 3.5 copy.122
  519.0 5.0 broadcast_multiply_fusion
  524.0 19.1 %reduce-scatter.2.cloned.1.call-done = f32[256,512]{1,0:T(8,128)} async-done(((f32[256,2048]{1,0:T(8,128)}), f32[256,512]{1,0:T(8,128)}) %reduce-scatter.2.cloned.1.call-update) | async-done | bytes 524304 | tf_op jit(solution)/shard_map/reduce_scatter | solution.py:118
  543.1 1.8 convert_bitcast_fusion
  (98 shorter events, 31.3 us)
Async XLA Ops:
  7.2 27.8 %copy-start = (bf16[512,2048]{1,0:T(8,128)(2,1)S(1)}, bf16[512,2048]{1,0:T(8,128)(2,1)}, u32[]{:S(2)}) copy-start(bf16[512,2048]{1,0:T(8,128)(2,1)} %param.9) | copy-start | bytes 6291460
  7.2 27.7 %all-gather.3.cloned.1.call-start = ((), (), s32[]{:S(2)}) async-start(), calls=%async_computation.10 | async-start | bytes 1310720 | tf_op jit(solution)/shard_map/all_gather | solution.py:122
  7.9 2.7 copy-start.19
  39.2 17.8 %all-to-all-start.4 = ((f32[1,256,512]{2,0,1:T(1,128)}), f32[1,256,512]{2,0,1:T(1,128)S(1)}, u32[]{:S(2)}, u32[]{:S(2)}) async-start(f32[1,256,512]{2,0,1:T(1,128)} %copy.104), calls=%async_computation.5 | async-start | bytes 1048576 | tf_op jit(solution)/shard_map/all_to_all | solution.py:38
  51.3 1.4 copy-start.5
  51.3 1.5 copy-start.6
  57.0 32.8 %all-to-all-start = ((f32[3,256,512]{2,0,1:T(4,128)}), f32[3,256,512]{2,0,1:T(4,128)}, u32[]{:S(2)}, u32[]{:S(2)}) async-start(f32[3,256,512]{2,0,1:T(4,128)} %copy.85), calls=%async_computation | async-start | bytes 4194304 | tf_op jit(solution)/shard_map/all_to_all | solution.py:38
  89.8 21.4 %all-to-all-start.5 = ((f32[2,256,512]{2,0,1:T(2,128)}), f32[2,256,512]{2,0,1:T(2,128)}, u32[]{:S(2)}, u32[]{:S(2)}) async-start(f32[2,256,512]{2,0,1:T(2,128)} %copy.110), calls=%async_computation.6 | async-start | bytes 2097152 | tf_op jit(solution)/shard_map/all_to_all | solution.py:38
  111.2 55.0 %all-to-all-start.1 = ((f32[6,256,512]{2,0,1:T(8,128)}), f32[6,256,512]{2,0,1:T(8,128)}, u32[]{:S(2)}, u32[]{:S(2)}) async-start(f32[6,256,512]{2,0,1:T(8,128)} %copy.92), calls=%async_computation.1 | async-start | bytes 8388608 | tf_op jit(solution)/shard_map/all_to_all | solution.py:38
  119.3 3.7 copy-start.11
  123.0 66.8 %copy-start.10 = (f32[1,256,512]{1,2,0:T(8,128)}, f32[1,256,512]{1,2,0:T(8,128)S(1)}, u32[]{:S(2)}) copy-start(f32[1,256,512]{1,2,0:T(8,128)S(1)} %fusion.15) | copy-start | bytes 1572868
  178.4 4.0 copy-start.1
  184.8 2.5 copy-start.2
  187.3 2.5 copy-start.12
  187.3 2.5 copy-start.22
  204.7 24.0 %all-to-all-start.2 = ((f32[2,256,512]{2,0,1:T(2,128)}), f32[2,256,512]{2,0,1:T(2,128)}, u32[]{:S(2)}, u32[]{:S(2)}) async-start(f32[2,256,512]{2,0,1:T(2,128)} %copy.95), calls=%async_computation.2 | async-start | bytes 2097152 | tf_op jit(solution)/shard_map/all_to_all | solution.py:38
  210.1 3.9 copy-start.8
  210.1 3.9 copy-start.9
  214.0 2.5 copy-start.13
  214.0 2.5 copy-start.14
  228.7 55.3 %all-to-all-start.6 = ((f32[6,256,512]{2,0,1:T(8,128)}), f32[6,256,512]{2,0,1:T(8,128)}, u32[]{:S(2)}, u32[]{:S(2)}) async-start(f32[6,256,512]{2,0,1:T(8,128)} %copy.111), calls=%async_computation.7 | async-start | bytes 8388608 | tf_op jit(solution)/shard_map/all_to_all | solution.py:38
  284.0 18.6 %all-to-all-start.3 = ((f32[1,256,512]{2,0,1:T(1,128)}), f32[1,256,512]{2,0,1:T(1,128)S(1)}, u32[]{:S(2)}, u32[]{:S(2)}) async-start(f32[1,256,512]{2,0,1:T(1,128)} %copy.101), calls=%async_computation.3 | async-start | bytes 1048576 | tf_op jit(solution)/shard_map/all_to_all | solution.py:38
  302.6 32.8 %all-to-all-start.7 = ((f32[3,256,512]{2,0,1:T(4,128)}), f32[3,256,512]{2,0,1:T(4,128)}, u32[]{:S(2)}, u32[]{:S(2)}) async-start(f32[3,256,512]{2,0,1:T(4,128)} %copy.117), calls=%async_computation.8 | async-start | bytes 4194304 | tf_op jit(solution)/shard_map/all_to_all | solution.py:38
  308.4 117.1 %all-reduce.7.cloned.1.call-start = ((), (), s32[]{:S(2)}) async-start(), calls=%async_computation.12 | async-start | bytes 2097152 | tf_op jit(solution)/shard_map/psum | solution.py:156
  339.6 1.1 copy-start.3
  340.8 1.2 copy-start.7
  340.8 1.2 copy-start.23
  341.9 169.6 %all-reduce.5.cloned.1.call-start = ((), (), s32[]{:S(2)}) async-start(), calls=%async_computation.11 | async-start | bytes 14680064 | tf_op jit(solution)/shard_map/psum | solution.py:155
  343.8 3.7 copy-start.15
  343.8 3.6 copy-start.17
  343.8 1.4 copy-start.20
  345.2 2.3 copy-start.4
  350.2 192.9 %reduce-scatter.2.cloned.1.call-start = ((), (), s32[]{:S(2)}) async-start(), calls=%async_computation.9 | async-start | bytes 2621440 | tf_op jit(solution)/shard_map/reduce_scatter | solution.py:118
  352.6 70.1 %copy-start.16 = (bf16[1,256,512]{1,2,0:T(8,128)(2,1)S(1)}, bf16[1,256,512]{1,2,0:T(8,128)(2,1)}, u32[]{:S(2)}) copy-start(bf16[1,256,512]{1,2,0:T(8,128)(2,1)} %copy-done.15) | copy-start | bytes 786436
  352.6 70.1 %copy-start.18 = (bf16[1,256,512]{1,2,0:T(8,128)(2,1)S(1)}, bf16[1,256,512]{1,2,0:T(8,128)(2,1)}, u32[]{:S(2)}) copy-start(bf16[1,256,512]{1,2,0:T(8,128)(2,1)} %copy-done.17) | copy-start | bytes 786436
  425.5 2.2 copy-start.21
Sparse Core Ops, SparseCore 0:
  9.7 25.2 all-gather.2
  342.0 47.4 all-reduce.6
  393.7 117.8 all-reduce.4
  513.8 29.2 reduce-scatter.1
where the time goes:
time: 559 us; the launch traced here: 552 us
  waiting for transfers between devices  258 us (46%)
  matrix products  69.8 us (12%)
  blocking collectives  69.5 us (12%)
  local copies, waits for them, and re-layouts  68 us (12%)
  starting transfers between devices  47.1 us (8%)
  other arithmetic  24.7 us (4%)
  between operations  14.8 us (3%)
    all_to_all x8, waiting for transfers between devices, regroup(): lax.all_to_all(stacked, 'seq', split_axis=1, concat_axis=1, tiled=True)  134 us
    psum x1, waiting for transfers between devices, on_device(): lax.psum((grad_win, grad_wout, grad_skip), ('seq', 'rep'))  82.8 us
    psum x1, blocking collectives, on_device(): lax.psum((grad_win, grad_wout, grad_skip), ('seq', 'rep'))  69.5 us
    dot_general x24, matrix products, table_apply(): return jnp.einsum(form, table, fields, precision=HIGHEST_PRECISION)  53.6 us
    all_to_all x8, starting transfers between devices, regroup(): lax.all_to_all(stacked, 'seq', split_axis=1, concat_axis=1, tiled=True)  46.6 us
    all_gather x1, waiting for transfers between devices, on_device(): piece = lax.all_gather(grad_rows, 'chan', axis=1, tiled=True)  21.2 us
    unnamed x61, local copies, waits for them, and re-layouts  20.4 us
    reduce_scatter x1, waiting for transfers between devices, on_device(): lax.psum_scatter(out_terms, 'chan', scatter_dimension=1, tiled=True)  19.1 us
  transfers between devices with their start and end apart: 12, of which 8 were waited for; matrix products, arithmetic and copies ran while one was open for 20% of the time, Pallas kernels for 0%

commit v1 on v0

--- a/solution.py
+++ b/solution.py
@@ -3,6 +3,7 @@
 import jax.numpy as jnp
 from jax import lax
 from jax.sharding import PartitionSpec as P
+from jax.lax import axis_index, axis_size, ppermute
 
 BLOCK = 512
 HIGHEST_PRECISION = lax.Precision.HIGHEST
@@ -119,7 +120,29 @@
         jnp.bfloat16
     )
     grad_rows = cotangent[0]
-    piece = lax.all_gather(grad_rows, "chan", axis=1, tiled=True)
+    ndev = axis_size("chan")
+    tray = []
+    u = 0
+    while u < ndev:
+        tray.append((u, (u + 1) % ndev))
+        u = u + 1
+    seen = []
+    u = 0
+    while u < ndev:
+        seen.append((u, (u - 1) % ndev))
+        u = u + 1
+    side_arr, near = ([grad_rows], [grad_rows])
+    for _ in range(ndev // 2):
+        w_next = ppermute(side_arr[-1], "chan", tray)
+        side_arr.append(w_next)
+    j = 0
+    while j < (ndev - 1) // 2:
+        all_rows = ppermute(near[-1], "chan", seen)
+        near.append(all_rows)
+        j = j + 1
+    frame_out = jnp.concatenate([*side_arr[::-1], *near[1:]], axis=1)
+    block_now = axis_index("chan")
+    piece = jnp.roll(frame_out, (block_now - ndev // 2) * grad_rows.shape[1], 1)
     grad_gated = lax.dot_general(
         piece, w_out, (((1,), (1,)), ((), ())), preferred_element_type=jnp.float32
     )

time: 559 us -> 530 us (0.948)
  waiting for transfers between devices: 258 us -> 224 us
    all_gather x1 -> x0, waiting for transfers between devices: 21.2 us -> none  [on_device(): piece = lax.all_gather(grad_rows, 'chan', axis=1, tiled=True)]
    reduce_scatter x1, waiting for transfers between devices: 19.1 us -> 0.01 us  [on_device(): lax.psum_scatter(out_terms, 'chan', scatter_dimension=1, tiled=True)]
    ppermute x0 -> x3, waiting for transfers between devices: none -> 9.05 us  [the longest x2 9.05 us: on_device(): w_next = ppermute(side_arr[-1], 'chan', tray)]
    unnamed x61 -> x74, local copies, waits for them, and re-layouts: 20.4 us -> 20.5 us
  transfers between devices with their start and end apart: 12 -> 14, of which waited for: 8 -> 8; matrix products, arithmetic and copies ran while one was open for 20% -> 21% of each run, Pallas kernels for 0% -> 0%
where the time goes in v1:
time: 530 us; the launch traced here: 522 us
  waiting for transfers between devices  224 us (42%)
  blocking collectives  70.1 us (13%)
  local copies, waits for them, and re-layouts  68.5 us (13%)
  matrix products  67.1 us (13%)
  starting transfers between devices  50.9 us (10%)
  other arithmetic  24.7 us (5%)
  between operations  16.6 us (3%)
    all_to_all x8, waiting for transfers between devices, regroup(): lax.all_to_all(stacked, 'seq', split_axis=1, concat_axis=1, tiled=True)  134 us
    psum x1, waiting for transfers between devices, on_device(): lax.psum((grad_win, grad_wout, grad_skip), ('seq', 'rep'))  80.9 us
    psum x1, blocking collectives, on_device(): lax.psum((grad_win, grad_wout, grad_skip), ('seq', 'rep'))  70.1 us
    dot_general x24, matrix products, table_apply(): return jnp.einsum(form, table, fields, precision=HIGHEST_PRECISION)  53.6 us
    all_to_all x8, starting transfers between devices, regroup(): lax.all_to_all(stacked, 'seq', split_axis=1, concat_axis=1, tiled=True)  46.9 us
    unnamed x74, local copies, waits for them, and re-layouts  20.5 us
  transfers between devices with their start and end apart: 14, of which 8 were waited for; matrix products, arithmetic and copies ran while one was open for 21% of the time, Pallas kernels for 0%

profile of v1, /device:TPU:1, one launch (start us, length us, event | category | flops | bytes accessed | tf_op | source)
XLA Modules:
  0.0 521.8 jit_solution(6308131110721262858)
XLA Ops:
  8.0 2.2 collective-permute-start
  11.7 2.6 copy.79
  14.3 3.4 collective-permute-done
  17.8 2.1 fusion.67
  19.8 5.6 %collective-permute-done.1 = bf16[256,512]{1,0:T(8,128)(2,1)S(1)} collective-permute-done((bf16[256,512]{1,0:T(8,128)(2,1)S(1)}, bf16[256,512]{1,0:T(8,128)(2,1)S(1)}, u32[]{:S(2)}, u32[]{:S(2)}) %collective-permute-start.1) | collective-permute-done | bytes 262176 | tf_op jit(solution)/shard_map/ppermute | solution.py:136
  28.5 8.3 %all-to-all-start.4 = ((f32[1,256,512]{2,0,1:T(1,128)}), f32[1,256,512]{2,0,1:T(1,128)S(1)}, u32[]{:S(2)}, u32[]{:S(2)}) async-start(f32[1,256,512]{2,0,1:T(1,128)} %copy.104), calls=%async_computation.5 | async-start | bytes 1048576 | tf_op jit(solution)/shard_map/all_to_all | solution.py:39
  36.8 2.0 copy.83
  38.8 2.0 copy.84
  43.6 2.9 copy.85
  46.5 5.7 %all-to-all-start = ((f32[3,256,512]{2,0,1:T(4,128)}), f32[3,256,512]{2,0,1:T(4,128)}, u32[]{:S(2)}, u32[]{:S(2)}) async-start(f32[3,256,512]{2,0,1:T(4,128)} %copy.85), calls=%async_computation | async-start | bytes 4194304 | tf_op jit(solution)/shard_map/all_to_all | solution.py:39
  55.2 1.8 copy.110
  57.0 22.3 %all-to-all-done = f32[3,256,512]{2,0,1:T(4,128)} async-done(((f32[3,256,512]{2,0,1:T(4,128)}), f32[3,256,512]{2,0,1:T(4,128)}, u32[]{:S(2)}, u32[]{:S(2)}) %all-to-all-start) | async-done | bytes 1572896 | tf_op jit(solution)/shard_map/all_to_all | solution.py:39
  79.3 5.7 %all-to-all-start.5 = ((f32[2,256,512]{2,0,1:T(2,128)}), f32[2,256,512]{2,0,1:T(2,128)}, u32[]{:S(2)}, u32[]{:S(2)}) async-start(f32[2,256,512]{2,0,1:T(2,128)} %copy.110), calls=%async_computation.6 | async-start | bytes 2097152 | tf_op jit(solution)/shard_map/all_to_all | solution.py:39
  85.0 2.1 copy.86
  87.1 2.5 fusion.9
  89.6 2.9 fusion
  93.1 1.8 copy.91
  94.9 3.9 copy.92
  98.8 1.9 all-to-all-done.5
  100.7 5.6 %all-to-all-start.1 = ((f32[6,256,512]{2,0,1:T(8,128)}), f32[6,256,512]{2,0,1:T(8,128)}, u32[]{:S(2)}, u32[]{:S(2)}) async-start(f32[6,256,512]{2,0,1:T(8,128)} %copy.92), calls=%async_computation.1 | async-start | bytes 8388608 | tf_op jit(solution)/shard_map/all_to_all | solution.py:39
  106.3 2.6 fusion.283
  109.0 1.8 fusion.30
  110.8 1.9 fusion.15
  112.7 2.6 fusion.26
  115.4 40.4 %all-to-all-done.1 = f32[6,256,512]{2,0,1:T(8,128)} async-done(((f32[6,256,512]{2,0,1:T(8,128)}), f32[6,256,512]{2,0,1:T(8,128)}, u32[]{:S(2)}, u32[]{:S(2)}) %all-to-all-start.1) | async-done | bytes 3145760 | tf_op jit(solution)/shard_map/all_to_all | solution.py:39
  155.8 6.6 %fusion.281 = (f32[3,256,512]{2,0,1:T(4,128)}, f32[3,256,512]{2,0,1:T(4,128)}) fusion(f32[6,256,512]{2,0,1:T(8,128)} %all-to-all-done.1), kind=kLoop, calls=%fused_computation.343 | loop fusion | bytes 6291456 | tf_op jit(solution)/shard_map/slice | solution.py:60
  162.3 2.7 copy.133
  165.0 2.9 copy.134
  167.9 4.0 fusion.63
  171.9 2.4 fusion.65
  174.3 2.5 subtract_bitcast_fusion.2
  176.9 2.5 add_bitcast_fusion.1
  179.4 3.8 fusion.279
  189.3 1.7 subtract_bitcast_fusion.3
  192.0 2.3 copy.95
  194.2 5.3 %all-to-all-start.2 = ((f32[2,256,512]{2,0,1:T(2,128)}), f32[2,256,512]{2,0,1:T(2,128)}, u32[]{:S(2)}, u32[]{:S(2)}) async-start(f32[2,256,512]{2,0,1:T(2,128)} %copy.95), calls=%async_computation.2 | async-start | bytes 2097152 | tf_op jit(solution)/shard_map/all_to_all | solution.py:39
  199.6 3.9 fusion.11
  203.5 2.4 fusion.20
  206.0 2.5 convolution_add_fusion
  208.5 2.7 subtract_bitcast_fusion.1
  211.2 1.9 pad_maximum_fusion.1
  213.1 5.2 copy.111
  218.2 5.8 %all-to-all-start.6 = ((f32[6,256,512]{2,0,1:T(8,128)}), f32[6,256,512]{2,0,1:T(8,128)}, u32[]{:S(2)}, u32[]{:S(2)}) async-start(f32[6,256,512]{2,0,1:T(8,128)} %copy.111), calls=%async_computation.7 | async-start | bytes 8388608 | tf_op jit(solution)/shard_map/all_to_all | solution.py:39
  224.0 2.6 fusion.282
  230.2 43.4 %all-to-all-done.6 = f32[6,256,512]{2,0,1:T(8,128)} async-done(((f32[6,256,512]{2,0,1:T(8,128)}), f32[6,256,512]{2,0,1:T(8,128)}, u32[]{:S(2)}, u32[]{:S(2)}) %all-to-all-start.6) | async-done | bytes 3145760 | tf_op jit(solution)/shard_map/all_to_all | solution.py:39
  273.5 4.6 all-to-all-start.3
  278.2 4.5 fusion.280
  283.2 2.5 fusion.2
  286.2 2.6 subtract_bitcast_fusion
  289.7 2.4 copy.117
  292.1 5.8 %all-to-all-start.7 = ((f32[3,256,512]{2,0,1:T(4,128)}), f32[3,256,512]{2,0,1:T(4,128)}, u32[]{:S(2)}, u32[]{:S(2)}) async-start(f32[3,256,512]{2,0,1:T(4,128)} %copy.117), calls=%async_computation.8 | async-start | bytes 4194304 | tf_op jit(solution)/shard_map/all_to_all | solution.py:39
  299.1 25.8 %all-to-all-done.7 = f32[3,256,512]{2,0,1:T(4,128)} async-done(((f32[3,256,512]{2,0,1:T(4,128)}), f32[3,256,512]{2,0,1:T(4,128)}, u32[]{:S(2)}, u32[]{:S(2)}) %all-to-all-start.7) | async-done | bytes 1572896 | tf_op jit(solution)/shard_map/all_to_all | solution.py:39
  324.9 2.7 copy.118
  331.5 1.8 fusion.56
  334.7 2.2 convolution_bitcast_fusion
  336.9 2.7 fusion.21
  340.0 2.1 fusion.290
  342.1 70.1 %psum.39 = f32[512]{0:T(512)S(1)} all-reduce(f32[512]{0:T(512)S(1)} %get-tuple-element.32), channel_id=1, replica_groups=mesh['seq'=16,'chan'=4,'rep'=2] {'seq','rep'}, use_global_device_ids=true, to_apply=%region_6.7 | all-reduce | flops 512 | bytes 4096 | tf_op jit(solution)/shard_map/psum | solution.py:178
  412.8 2.7 fusion.19
  418.7 80.9 %all-reduce.5.cloned.1.call-done = (f32[512,1536]{0,1:T(8,128)}, f32[512,2048]{1,0:T(8,128)}) async-done(((f32[512,1536]{0,1:T(8,128)}, f32[512,2048]{1,0:T(8,128)}), (f32[512,1536]{0,1:T(8,128)}, f32[512,2048]{1,0:T(8,128)})) %all-reduce.5.cloned.1.call-update) | async-done | bytes 7340048 | tf_op jit(solution)/shard_map/psum | solution.py:178
  499.7 3.9 broadcast_multiply_fusion.1
  503.6 3.5 copy.122
  507.1 5.0 broadcast_multiply_fusion
  512.1 1.8 convert_bitcast_fusion
  (115 shorter events, 33.9 us)
Async XLA Ops:
  8.0 17.8 %copy-start = (bf16[512,2048]{1,0:T(8,128)(2,1)S(1)}, bf16[512,2048]{1,0:T(8,128)(2,1)}, u32[]{:S(2)}) copy-start(bf16[512,2048]{1,0:T(8,128)(2,1)} %param.9) | copy-start | bytes 6291460
  8.0 9.7 %collective-permute-start = (bf16[256,512]{1,0:T(8,128)(2,1)}, bf16[256,512]{1,0:T(8,128)(2,1)S(1)}, u32[]{:S(2)}, u32[]{:S(2)}) collective-permute-start(bf16[256,512]{1,0:T(8,128)(2,1)} %bitcast.270), channel_id=1, source_target_pairs={{0,2},{2,4},{4,6},{6,0},{1,3},{3,5},{5,7},{7,1},{8,10},{10,12},{12... | collective-permute-start | bytes 786440 | tf_op jit(solution)/shard_map/ppermute | solution.py:136
  10.2 15.4 %collective-permute-start.2 = (bf16[256,512]{1,0:T(8,128)(2,1)}, bf16[256,512]{1,0:T(8,128)(2,1)S(1)}, u32[]{:S(2)}, u32[]{:S(2)}) collective-permute-start(bf16[256,512]{1,0:T(8,128)(2,1)} %bitcast.271), channel_id=1, source_target_pairs={{0,6},{2,0},{4,2},{6,4},{1,7},{3,1},{5,3},{7,5},{8,14},{10,8},{12,... | collective-permute-start | bytes 786440 | tf_op jit(solution)/shard_map/ppermute | solution.py:140
  11.7 6.0 %copy-start.22 = (bf16[1,256,512]{2,1,0:T(8,128)(2,1)S(1)}, bf16[1,256,512]{2,1,0:T(8,128)(2,1)}, u32[]{:S(2)}) copy-start(bf16[1,256,512]{2,1,0:T(8,128)(2,1)} %param.7) | copy-start | bytes 786436
  17.8 7.7 %collective-permute-start.1 = (bf16[256,512]{1,0:T(8,128)(2,1)S(1)}, bf16[256,512]{1,0:T(8,128)(2,1)S(1)}, u32[]{:S(2)}, u32[]{:S(2)}) collective-permute-start(bf16[256,512]{1,0:T(8,128)(2,1)S(1)} %collective-permute-done), channel_id=1, source_target_pairs={{0,2},{2,4},{4,6},{6,0},{1,3},{3,5},{5,7},{7,1},{8,10},{10,12},{12... | collective-permute-start | bytes 786440 | tf_op jit(solution)/shard_map/ppermute | solution.py:136
  17.8 7.8 %copy-start.17 = (bf16[1,256,512]{2,1,0:T(8,128)(2,1)S(1)}, bf16[1,256,512]{2,1,0:T(8,128)(2,1)}, u32[]{:S(2)}) copy-start(bf16[1,256,512]{2,1,0:T(8,128)(2,1)} %param.13) | copy-start | bytes 786436
  19.8 5.9 %copy-start.1 = (f32[3,512,256]{2,1,0:T(8,128)}, f32[3,512,256]{2,1,0:T(8,128)S(1)}, u32[]{:S(2)}) copy-start(f32[3,512,256]{2,1,0:T(8,128)S(1)} %fusion.67) | copy-start | bytes 4718596
  25.7 1.7 copy-start.5
  28.5 18.1 %all-to-all-start.4 = ((f32[1,256,512]{2,0,1:T(1,128)}), f32[1,256,512]{2,0,1:T(1,128)S(1)}, u32[]{:S(2)}, u32[]{:S(2)}) async-start(f32[1,256,512]{2,0,1:T(1,128)} %copy.104), calls=%async_computation.5 | async-start | bytes 1048576 | tf_op jit(solution)/shard_map/all_to_all | solution.py:39
  40.9 1.4 copy-start.7
  40.9 1.5 copy-start.8
  46.5 32.8 %all-to-all-start = ((f32[3,256,512]{2,0,1:T(4,128)}), f32[3,256,512]{2,0,1:T(4,128)}, u32[]{:S(2)}, u32[]{:S(2)}) async-start(f32[3,256,512]{2,0,1:T(4,128)} %copy.85), calls=%async_computation | async-start | bytes 4194304 | tf_op jit(solution)/shard_map/all_to_all | solution.py:39
  79.3 21.4 %all-to-all-start.5 = ((f32[2,256,512]{2,0,1:T(2,128)}), f32[2,256,512]{2,0,1:T(2,128)}, u32[]{:S(2)}, u32[]{:S(2)}) async-start(f32[2,256,512]{2,0,1:T(2,128)} %copy.110), calls=%async_computation.6 | async-start | bytes 2097152 | tf_op jit(solution)/shard_map/all_to_all | solution.py:39
  100.7 55.0 %all-to-all-start.1 = ((f32[6,256,512]{2,0,1:T(8,128)}), f32[6,256,512]{2,0,1:T(8,128)}, u32[]{:S(2)}, u32[]{:S(2)}) async-start(f32[6,256,512]{2,0,1:T(8,128)} %copy.92), calls=%async_computation.1 | async-start | bytes 8388608 | tf_op jit(solution)/shard_map/all_to_all | solution.py:39
  109.0 3.7 copy-start.13
  112.7 66.7 %copy-start.12 = (f32[1,256,512]{1,2,0:T(8,128)}, f32[1,256,512]{1,2,0:T(8,128)S(1)}, u32[]{:S(2)}) copy-start(f32[1,256,512]{1,2,0:T(8,128)S(1)} %fusion.15) | copy-start | bytes 1572868
  167.9 4.0 copy-start.2
  174.3 2.5 copy-start.3
  176.8 2.5 copy-start.14
  176.9 2.5 copy-start.25
  194.2 24.0 %all-to-all-start.2 = ((f32[2,256,512]{2,0,1:T(2,128)}), f32[2,256,512]{2,0,1:T(2,128)}, u32[]{:S(2)}, u32[]{:S(2)}) async-start(f32[2,256,512]{2,0,1:T(2,128)} %copy.95), calls=%async_computation.2 | async-start | bytes 2097152 | tf_op jit(solution)/shard_map/all_to_all | solution.py:39
  199.6 3.9 copy-start.10
  199.6 3.9 copy-start.11
  203.5 2.5 copy-start.15
  203.5 2.5 copy-start.16
  218.2 55.3 %all-to-all-start.6 = ((f32[6,256,512]{2,0,1:T(8,128)}), f32[6,256,512]{2,0,1:T(8,128)}, u32[]{:S(2)}, u32[]{:S(2)}) async-start(f32[6,256,512]{2,0,1:T(8,128)} %copy.111), calls=%async_computation.7 | async-start | bytes 8388608 | tf_op jit(solution)/shard_map/all_to_all | solution.py:39
  273.5 18.6 %all-to-all-start.3 = ((f32[1,256,512]{2,0,1:T(1,128)}), f32[1,256,512]{2,0,1:T(1,128)S(1)}, u32[]{:S(2)}, u32[]{:S(2)}) async-start(f32[1,256,512]{2,0,1:T(1,128)} %copy.101), calls=%async_computation.3 | async-start | bytes 1048576 | tf_op jit(solution)/shard_map/all_to_all | solution.py:39
  292.1 32.8 %all-to-all-start.7 = ((f32[3,256,512]{2,0,1:T(4,128)}), f32[3,256,512]{2,0,1:T(4,128)}, u32[]{:S(2)}, u32[]{:S(2)}) async-start(f32[3,256,512]{2,0,1:T(4,128)} %copy.117), calls=%async_computation.8 | async-start | bytes 4194304 | tf_op jit(solution)/shard_map/all_to_all | solution.py:39
  297.9 117.6 %all-reduce.7.cloned.1.call-start = ((), (), s32[]{:S(2)}) async-start(), calls=%async_computation.11 | async-start | bytes 2097152 | tf_op jit(solution)/shard_map/psum | solution.py:179
  329.2 1.1 copy-start.4
  330.3 1.2 copy-start.9
  330.3 1.2 copy-start.26
  331.4 168.2 %all-reduce.5.cloned.1.call-start = ((), (), s32[]{:S(2)}) async-start(), calls=%async_computation.10 | async-start | bytes 14680064 | tf_op jit(solution)/shard_map/psum | solution.py:178
  333.3 3.7 copy-start.18
  333.3 3.6 copy-start.20
  333.3 1.4 copy-start.23
  334.7 2.3 copy-start.6
  339.7 172.4 %reduce-scatter.2.cloned.1.call-start = ((), (), s32[]{:S(2)}) async-start(), calls=%async_computation.9 | async-start | bytes 2621440 | tf_op jit(solution)/shard_map/reduce_scatter | solution.py:119
  342.1 70.7 %copy-start.19 = (bf16[1,256,512]{1,2,0:T(8,128)(2,1)S(1)}, bf16[1,256,512]{1,2,0:T(8,128)(2,1)}, u32[]{:S(2)}) copy-start(bf16[1,256,512]{1,2,0:T(8,128)(2,1)} %copy-done.18) | copy-start | bytes 786436
  342.1 70.7 %copy-start.21 = (bf16[1,256,512]{1,2,0:T(8,128)(2,1)S(1)}, bf16[1,256,512]{1,2,0:T(8,128)(2,1)}, u32[]{:S(2)}) copy-start(bf16[1,256,512]{1,2,0:T(8,128)(2,1)} %copy-done.20) | copy-start | bytes 786436
  415.5 2.2 copy-start.24
Sparse Core Ops, SparseCore 0:
  331.5 46.0 all-reduce.6
  381.7 117.8 all-reduce.4
Sparse Core Ops, SparseCore 1:
  342.6 26.8 reduce-scatter.1
